TPU v7x, 32 devices: a whole 2x2x4 slice. The times are simulated.
32 devices in a mesh: groups: 2 (over y), ctx: 8 (over z, x), tp: 2 (over core).
Axes of the slice: x: 2, y: 2, z: 4, core: 2. Of those that a mesh axis runs over, the one named last changes fastest.
Arguments:
- tokens: bfloat16 [4096, 2688], P(('groups', 'ctx', 'tp')), parts along dimension 0, may hold values from -6 to 6
- output_gradient: bfloat16 [4096, 2688], P(('groups', 'ctx', 'tp')), parts along dimension 0, may hold values from -6 to 6
- document_index: int32 [4096], P(('groups', 'ctx')), parts along dimension 0, may hold values from 0 to 3, never falling along the last dimension, each value on 1 to 1024 neighbouring positions
- real_token_count: int32 [16], P(('groups', 'ctx')), parts along dimension 0, may hold values from 64 to 256, as said below
- input_norm_gain: float32 [2688], replicated, may hold values from 0.1 to 1.9
- query_norm_gain: float32 [128], replicated, may hold values from 0.1 to 1.9
- key_norm_gain: float32 [128], replicated, may hold values from 0.1 to 1.9
- output_norm_gain: float32 [2688], replicated, may hold values from 0.1 to 1.9
- query_projection: bfloat16 [2688, 512], P(None, 'tp'), may hold values from -0.125 to 0.125
- key_projection: bfloat16 [2688, 256], P(None, 'tp'), may hold values from -0.125 to 0.125
- value_projection: bfloat16 [2688, 256], P(None, 'tp'), may hold values from -0.125 to 0.125
- output_projection: bfloat16 [512, 2688], P('tp'), may hold values from -0.25 to 0.25
- adapter_down_maps: bfloat16 [2688, 48], replicated, may hold values from -0.125 to 0.125
- adapter_query_up: bfloat16 [16, 512], P(None, 'tp'), may hold values from -0.375 to 0.375
- adapter_key_up: bfloat16 [16, 256], P(None, 'tp'), may hold values from -0.375 to 0.375
- adapter_value_up: bfloat16 [16, 256], P(None, 'tp'), may hold values from -0.375 to 0.375
- adapter_output_down: bfloat16 [512, 16], P('tp'), may hold values from -0.25 to 0.25
- adapter_output_up: bfloat16 [16, 2688], replicated, may hold values from -0.375 to 0.375
Outputs:
- layer_out: bfloat16 [4096, 2688], P(('groups', 'ctx', 'tp')), parts along dimension 0
- grad_in: bfloat16 [4096, 2688], P(('groups', 'ctx', 'tp')), parts along dimension 0
- grad_down: float32 [5376, 48], P(('groups', 'tp')), parts along dimension 0
- query_up_gradient: float32 [32, 512], P('groups', 'tp'), parts along dimension 0
- key_up_gradient: float32 [32, 256], P('groups', 'tp'), parts along dimension 0
- value_up_gradient: float32 [32, 256], P('groups', 'tp'), parts along dimension 0
- grad_down_out: float32 [1024, 16], P(('groups', 'tp')), parts along dimension 0
- output_up_gradient: float32 [32, 2688], P('groups', 'tp'), parts along dimension 0
There are 2 independent parts, one for each index of `groups`. A program takes and returns all parts, laid end to end along the dimension named above; an argument that names none is the same for every part. Nothing has to cross between parts.
Inputs may be any that keep to these rules, and one draw needn't show every extreme that they name: `document_index`: document numbers never fall along the tokens; a document has 1 to 1024 tokens and one has exactly that many. `real_token_count`: the real tokens of a block come first and the rest is padding; some block is full and some holds 64 real tokens.
All inputs are finite; a program needn't handle non-finite values.
Results may differ from a plain program's by a relative error of at most 0.034.
Values may be sent and summed in bfloat16 or wider, within the bound.
No kernel may reach another device: no remote copies, remote signals or barrier semaphores. Data moves between devices by JAX's collectives and lax.ppermute only.
A program may use at most 64 MiB of HBM per device.

v0:
```python
import jax
import jax.numpy as jnp
from jax import lax
from jax.sharding import PartitionSpec as P

WINDOW = 1024
epsilon = 1e-06
adapter_scale = 2.0
score_scale = 168.0 ** (-0.5)


def passed_along(value, axis, steps):
    count = lax.axis_size(axis)
    leading, last = (max(0, -steps), min(count, count - steps))
    return lax.ppermute(value, axis, [(source, source + steps) for source in range(leading, last)])


def norm_rows(source, gain_vec):
    inverse = lax.rsqrt(jnp.mean(source * source, axis=-1, keepdims=True) + epsilon)
    return source * inverse * gain_vec


def norm_back(source, gain_vec, incoming):
    inverse = lax.rsqrt(jnp.mean(source * source, axis=-1, keepdims=True) + epsilon)
    scaled = source * inverse
    upward = incoming * gain_vec
    return inverse * (upward - scaled * jnp.mean(upward * scaled, axis=-1, keepdims=True))


def matrix_product(first_op, second_op):
    return jnp.dot(first_op, second_op, preferred_element_type=jnp.float32)


def multiply_by_transpose(first_op, second_op):
    return lax.dot_general(
        first_op, second_op, (((1,), (1,)), ((), ())), preferred_element_type=jnp.float32
    )


def transpose_multiply(first_op, second_op):
    return lax.dot_general(
        first_op, second_op, (((0,), (0,)), ((), ())), preferred_element_type=jnp.float32
    )


def window_mask(query_segs, key_codes):
    query_count = query_segs.shape[0]
    key_total = key_codes.shape[0]
    distance = (key_total - query_count + jnp.arange(query_count))[:, None] - jnp.arange(key_total)[
        None, :
    ]
    same_doc = key_codes[None, :] == query_segs[:, None] + 1
    return (distance == 0) | (distance > 0) & (distance < WINDOW) & same_doc


def on_device(
    tokens,
    output_gradient,
    document_index,
    real_token_count,
    input_norm_gain,
    query_norm_gain,
    key_norm_gain,
    output_norm_gain,
    query_projection,
    key_projection,
    value_projection,
    output_projection,
    adapter_down_maps,
    adapter_query_up,
    adapter_key_up,
    adapter_value_up,
    adapter_output_down,
    adapter_output_up,
):
    row_count, model_width = tokens.shape
    shard_len = document_index.shape[0]
    head_dim = key_projection.shape[1]
    adapter_product = adapter_key_up.shape[0]
    heads_here = query_projection.shape[1] // head_dim
    ctx_size = lax.axis_size("ctx")
    tp_index = lax.axis_index("tp")
    slice_width = model_width // lax.axis_size("tp")
    reach_shards = WINDOW // shard_len
    send_count = min(reach_shards, ctx_size - 1)
    tok_float = tokens.astype(jnp.float32)
    normed_rows = norm_rows(tok_float, input_norm_gain).astype(jnp.bfloat16)
    normalized_input = lax.all_gather(normed_rows, "tp", axis=0, tiled=True)
    middle_list = matrix_product(normalized_input, adapter_down_maps).astype(jnp.bfloat16)
    middle_query = middle_list[:, :adapter_product]
    middle_key = middle_list[:, adapter_product : 2 * adapter_product]
    middle_value = middle_list[:, 2 * adapter_product :]
    query_before_norm = matrix_product(
        normalized_input, query_projection
    ) + adapter_scale * matrix_product(middle_query, adapter_query_up)
    key_before_norm = matrix_product(
        normalized_input, key_projection
    ) + adapter_scale * matrix_product(middle_key, adapter_key_up)
    value_before_norm = matrix_product(
        normalized_input, value_projection
    ) + adapter_scale * matrix_product(middle_value, adapter_value_up)
    query_heads = query_before_norm.reshape(shard_len, heads_here, head_dim)
    query_normed = norm_rows(query_heads, query_norm_gain).astype(jnp.bfloat16)
    key_normed = norm_rows(key_before_norm, key_norm_gain).astype(jnp.bfloat16)
    value_cast = value_before_norm.astype(jnp.bfloat16)
    positions = jnp.arange(shard_len)
    is_valid = positions < real_token_count[0]
    valid_rows = is_valid.astype(jnp.float32)
    local_codes = jnp.where(is_valid, document_index + 1, 0)
    local_pair = jnp.concatenate([key_normed, value_cast], axis=1)
    received = []
    for hop_index in range(1, send_count + 1):
        received.append(passed_along((local_pair, local_codes), "ctx", hop_index))
    missing = reach_shards - send_count
    blank_pair = jnp.zeros_like(local_pair)
    blank_codes = jnp.zeros_like(local_codes)
    earlier = [(blank_pair, blank_codes)] * missing + list(reversed(received))
    key_pairs = jnp.concatenate([entry[0] for entry in earlier] + [local_pair], axis=0)
    key_codes_all = jnp.concatenate([entry[1] for entry in earlier] + [local_codes], axis=0)
    keys_all = key_pairs[:, :head_dim]
    values_all = key_pairs[:, head_dim:]
    allowed = window_mask(document_index, key_codes_all)
    scores = (
        jnp.einsum("thd,sd->hts", query_normed, keys_all, preferred_element_type=jnp.float32)
        * score_scale
    )
    weights = jnp.where(allowed[None], jnp.exp(scores), 0.0)
    attn_probs = weights / jnp.sum(weights, axis=-1, keepdims=True)
    probs_cast = attn_probs.astype(jnp.bfloat16)
    attention_result = jnp.einsum(
        "hts,sd->thd", probs_cast, values_all, preferred_element_type=jnp.float32
    )
    attention_result = (
        (attention_result * valid_rows[:, None, None])
        .astype(jnp.bfloat16)
        .reshape(shard_len, heads_here * head_dim)
    )
    part_out = matrix_product(attention_result, output_projection)
    partial_middle = matrix_product(attention_result, adapter_output_down)
    output_total, mid_sum = (
        lax.psum_scatter(
            part_out.astype(jnp.bfloat16), "tp", scatter_dimension=0, tiled=True
        ).astype(jnp.float32),
        lax.psum_scatter(
            partial_middle.astype(jnp.bfloat16), "tp", scatter_dimension=0, tiled=True
        ).astype(jnp.float32),
    )
    middle_output = mid_sum.astype(jnp.bfloat16)
    apply_prenorm = output_total + adapter_scale * matrix_product(middle_output, adapter_output_up)
    layer_out = norm_rows(apply_prenorm, output_norm_gain).astype(jnp.bfloat16)
    prenorm_gradient = norm_back(
        apply_prenorm, output_norm_gain, output_gradient.astype(jnp.float32)
    ).astype(jnp.bfloat16)
    middle_output_gradient = (
        adapter_scale * multiply_by_transpose(prenorm_gradient, adapter_output_up)
    ).astype(jnp.bfloat16)
    complete_gradient, middle_complete_gradient, middle_complete = (
        lax.all_gather(prenorm_gradient, "tp", axis=0, tiled=True),
        lax.all_gather(middle_output_gradient, "tp", axis=0, tiled=True),
        lax.all_gather(middle_output, "tp", axis=0, tiled=True),
    )
    gradient_portion = lax.dynamic_slice_in_dim(
        complete_gradient, tp_index * slice_width, slice_width, 1
    )
    output_up_contribution = adapter_scale * transpose_multiply(middle_complete, gradient_portion)
    attention_gradient = multiply_by_transpose(
        complete_gradient, output_projection
    ) + multiply_by_transpose(middle_complete_gradient, adapter_output_down)
    attention_gradient = (attention_gradient * valid_rows[:, None]).astype(jnp.bfloat16)
    down_out_term = transpose_multiply(attention_result, middle_complete_gradient)
    grad_heads = attention_gradient.reshape(shard_len, heads_here, head_dim)
    grad_probs = jnp.einsum(
        "thd,sd->hts", grad_heads, values_all, preferred_element_type=jnp.float32
    )
    inner_sum = jnp.sum(attn_probs * grad_probs, axis=-1, keepdims=True)
    grad_scores = (attn_probs * (grad_probs - inner_sum) * score_scale).astype(jnp.bfloat16)
    grad_query = jnp.einsum(
        "hts,sd->thd", grad_scores, keys_all, preferred_element_type=jnp.float32
    )
    grad_keys = jnp.einsum(
        "hts,thd->sd", grad_scores, query_normed, preferred_element_type=jnp.float32
    )
    grad_values = jnp.einsum(
        "hts,thd->sd", probs_cast, grad_heads, preferred_element_type=jnp.float32
    )
    grad_pairs = jnp.concatenate([grad_keys, grad_values], axis=1)
    own_grads = grad_pairs[reach_shards * shard_len :]
    for hop_index in range(1, send_count + 1):
        own_grads = own_grads + passed_along(
            grad_pairs[
                (reach_shards - hop_index) * shard_len : (reach_shards - hop_index + 1) * shard_len
            ].astype(jnp.bfloat16),
            "ctx",
            -hop_index,
        ).astype(jnp.float32)
    query_prenorm_gradient = (
        norm_back(query_heads, query_norm_gain, grad_query)
        .reshape(shard_len, heads_here * head_dim)
        .astype(jnp.bfloat16)
    )
    key_prenorm_gradient = norm_back(
        key_before_norm, key_norm_gain, own_grads[:, :head_dim]
    ).astype(jnp.bfloat16)
    value_prenorm_gradient = own_grads[:, head_dim:].astype(jnp.bfloat16)
    query_up_contribution = adapter_scale * transpose_multiply(middle_query, query_prenorm_gradient)
    key_up_contribution = adapter_scale * transpose_multiply(middle_key, key_prenorm_gradient)
    value_up_contribution = adapter_scale * transpose_multiply(middle_value, value_prenorm_gradient)
    middle_gradients = jnp.concatenate(
        [
            adapter_scale * multiply_by_transpose(query_prenorm_gradient, adapter_query_up),
            adapter_scale * multiply_by_transpose(key_prenorm_gradient, adapter_key_up),
            adapter_scale * multiply_by_transpose(value_prenorm_gradient, adapter_value_up),
        ],
        axis=1,
    ).astype(jnp.bfloat16)
    grad_normed = (
        multiply_by_transpose(query_prenorm_gradient, query_projection)
        + multiply_by_transpose(key_prenorm_gradient, key_projection)
        + multiply_by_transpose(value_prenorm_gradient, value_projection)
        + multiply_by_transpose(middle_gradients, adapter_down_maps)
    )
    grad_normed_rows = lax.psum_scatter(
        grad_normed.astype(jnp.bfloat16), "tp", scatter_dimension=0, tiled=True
    ).astype(jnp.float32)
    grad_in = norm_back(tok_float, input_norm_gain, grad_normed_rows).astype(jnp.bfloat16)
    down_term = lax.psum_scatter(
        transpose_multiply(normalized_input, middle_gradients).astype(jnp.bfloat16),
        "tp",
        scatter_dimension=0,
        tiled=True,
    )
    adapter_totals = (
        lax.psum(down_term, "ctx").astype(jnp.float32),
        lax.psum(query_up_contribution.astype(jnp.bfloat16), "ctx").astype(jnp.float32),
        lax.psum(key_up_contribution.astype(jnp.bfloat16), "ctx").astype(jnp.float32),
        lax.psum(value_up_contribution.astype(jnp.bfloat16), "ctx").astype(jnp.float32),
        lax.psum(down_out_term.astype(jnp.bfloat16), "ctx").astype(jnp.float32),
        lax.psum(output_up_contribution.astype(jnp.bfloat16), "ctx").astype(jnp.float32),
    )
    return (
        layer_out,
        grad_in,
        adapter_totals[0],
        adapter_totals[1],
        adapter_totals[2],
        adapter_totals[3],
        adapter_totals[4],
        adapter_totals[5],
    )


def solution(mesh):
    in_specs = (
        P(("groups", "ctx", "tp"), None),
        P(("groups", "ctx", "tp"), None),
        P(("groups", "ctx")),
        P(("groups", "ctx")),
        P(),
        P(),
        P(),
        P(),
        P(None, "tp"),
        P(None, "tp"),
        P(None, "tp"),
        P("tp", None),
        P(),
        P(None, "tp"),
        P(None, "tp"),
        P(None, "tp"),
        P("tp", None),
        P(),
    )
    out_specs = (
        P(("groups", "ctx", "tp"), None),
        P(("groups", "ctx", "tp"), None),
        P(("groups", "tp"), None),
        P("groups", "tp"),
        P("groups", "tp"),
        P("groups", "tp"),
        P(("groups", "tp"), None),
        P("groups", "tp"),
    )
    return jax.shard_map(
        on_device, mesh=mesh, in_specs=in_specs, out_specs=out_specs, check_vma=False
    )
```

profile of v0, /device:TPU:0, one launch (start us, length us, event | category | flops | bytes accessed | tf_op | source)
XLA Modules:
  0.0 319.8 jit_solution(16461796081767223556)
XLA Ops:
  9.2 2.2 fusion.21
  12.2 5.9 %collective-permute-start.4 = (s32[256]{0:T(256)S(1)}, s32[256]{0:T(256)S(1)}, u32[]{:S(2)}, u32[]{:S(2)}) collective-permute-start(s32[256]{0:T(256)S(1)} %get-tuple-element.19), channel_id=1, source_target_pairs={{0,8},{2,10},{4,12},{6,14},{1,9},{3,11},{5,13},{7,15},{16,24},{18,... | collective-permute-start | bytes 3080 | tf_op jit(solution)/shard_map/ppermute | solution.py:15
  18.1 4.4 %collective-permute-start.5 = (s32[256]{0:T(256)S(1)}, s32[256]{0:T(256)S(1)}, u32[]{:S(2)}, u32[]{:S(2)}) collective-permute-start(s32[256]{0:T(256)S(1)} %get-tuple-element.19), channel_id=1, source_target_pairs={{0,6},{2,8},{4,10},{6,12},{8,14},{1,7},{3,9},{5,11},{7,13},{9,15},... | collective-permute-start | bytes 3080 | tf_op jit(solution)/shard_map/ppermute | solution.py:15
  23.8 3.1 collective-permute-start.7
  29.5 2.0 convolution_convert_fusion.2
  33.5 3.9 %collective-permute-start = (bf16[256,256]{0,1:T(8,128)(2,1)S(1)}, bf16[256,256]{0,1:T(8,128)(2,1)S(1)}, u32[]{:S(2)}, u32[]{:S(2)}) collective-permute-start(bf16[256,256]{0,1:T(8,128)(2,1)S(1)} %pad_maximum_fusion.1), channel_id=1, source_target_pairs={{0,8},{2,10},{4,12},{6,14},{1,9},{3,11},{5,13},{7,15},{16,24},{18,... | collective-permute-start | bytes 393224 | tf_op jit(solution)/shard_map/ppermute | solution.py:15
  38.7 1.9 collective-permute-start.2
  40.5 2.8 collective-permute-start.3
  47.9 3.4 %fusion.31 = f32[2,256,1280]{1,2,0:T(8,128)} fusion(pred[256,1280]{0,1:T(8,128)(4,1)S(1)} %copy-done.21, bf16[1280,256]{0,1:T(8,128)(2,1)} %constant_dynamic-update-slice_fusion, f32[256,256]{0,1:T(8,128)S(1)} %get-tuple-element.24, f32[128]{0:T(128)S(1)} %copy-done.43, f32[256,2]{0,1:T(2,128)S(1)} %add_rsqrt_fusion), kind=kOutput, calls=%fused_computation.49 | convolution fusion | flops 169936640 | bytes 3541504 | tf_op jit(solution)/shard_map/div | solution.py:128
  51.3 2.2 fusion.46
  54.5 3.0 convolution_convert_fusion
  57.6 8.8 %reduce-scatter.13.cloned.1.call-done = bf16[128,16]{1,0:T(8,128)(2,1)} async-done(((bf16[256,16]{1,0:T(8,128)(2,1)}), bf16[128,16]{1,0:T(8,128)(2,1)}) %reduce-scatter.13.cloned.1.call-update) | async-done | bytes 4112
  66.4 12.3 %reduce-scatter.9.cloned.1.call-done = bf16[128,2688]{1,0:T(8,128)(2,1)} async-done(((bf16[256,2688]{1,0:T(8,128)(2,1)}), bf16[128,2688]{1,0:T(8,128)(2,1)}) %reduce-scatter.9.cloned.1.call-update) | async-done | bytes 688144 | tf_op jit(solution)/shard_map/reduce_scatter | solution.py:141
  83.1 1.8 all_gather.15
  86.2 1.9 all_gather.14
  89.1 4.0 %all-gather.5.cloned.1.call-done = bf16[256,2688]{1,0:T(8,128)(2,1)} async-done(((bf16[128,2688]{1,0:T(8,128)(2,1)}), bf16[256,2688]{1,0:T(8,128)(2,1)}) %all-gather.5.cloned.1.call-update) | async-done | bytes 1376272 | tf_op jit(solution)/shard_map/all_gather | solution.py:158
  93.1 2.3 fusion.45
  95.4 3.2 convolution_bitcast_fusion
  99.3 5.7 %multiply_reduce_fusion.3 = (f32[256,2]{0,1:T(2,128)S(1)}, f32[256,2,128]{0,2,1:T(8,128)}) fusion(f32[256,256]{0,1:T(8,128)} %copy-done.18, f32[256,2]{0,1:T(2,128)S(1)} %copy-done.37, f32[128]{0:T(128)S(1)} %copy-done.44, f32[2,256,1280]{1,2,0:T(8,128)} %fusion.31, f32[2,256,1280]{1,2,0:T(8,128)} %convolution_bitcast_fusion, ...), kind=kOutput, calls=%fused_computation.99 | convolution fusion | flops 171312384 | bytes 11342336 | tf_op jit(solution)/shard_map/hts,sd->thd/dot_general | solution.py:177
  105.0 5.7 %convolution_bitcast_fusion.2 = f32[1280,128]{0,1:T(8,128)} fusion(f32[2,256,1280]{1,2,0:T(8,128)} %fusion.31, f32[2,256,1280]{1,2,0:T(8,128)} %convolution_bitcast_fusion, f32[256,256]{0,1:T(8,128)} %copy-done.18, f32[128]{0:T(128)S(1)} %copy-done.44, f32[256,2]{0,1:T(2,128)S(1)} %copy-done.37), kind=kOutput, calls=%fused_computation.19 | convolution fusion | flops 171247360 | bytes 6162944 | tf_op jit(solution)/shard_map/hts,thd->sd/dot_general | solution.py:180
  112.7 2.1 fusion.83
  121.7 2.0 collective-permute-done.10
  123.7 10.1 %collective-permute-done.11 = bf16[256,256]{0,1:T(8,128)(2,1)S(1)} collective-permute-done((bf16[256,256]{0,1:T(8,128)(2,1)S(1)}, bf16[256,256]{0,1:T(8,128)(2,1)S(1)}, u32[]{:S(2)}, u32[]{:S(2)}) %collective-permute-start.11) | collective-permute-done | bytes 131104 | tf_op jit(solution)/shard_map/ppermute | solution.py:15
  136.9 2.1 copy.54
  139.8 3.9 %convolution_add_fusion.1 = f32[256,2688]{1,0:T(8,128)} fusion(f32[256,2688]{1,0:T(8,128)} %fusion.83, bf16[256,128]{0,1:T(8,128)(2,1)S(1)} %multiply_convert_fusion.4, bf16[2688,128]{1,0:T(8,128)(2,1)S(1)} %copy-done.8), kind=kOutput, calls=%fused_computation.2 | convolution fusion | flops 176848896 | bytes 6258688 | tf_op jit(solution)/shard_map/dot_general | solution.py:35
  143.8 2.1 fusion.63
  145.9 3.6 %reduce-scatter.15.cloned.1.call-done = bf16[1344,48]{1,0:T(8,128)(2,1)} async-done(((bf16[2688,48]{1,0:T(8,128)(2,1)}), bf16[1344,48]{1,0:T(8,128)(2,1)}) %reduce-scatter.15.cloned.1.call-update) | async-done | bytes 129040
  149.5 1.8 copy.55
  151.4 4.3 %fusion.2 = bf16[256,2688]{1,0:T(8,128)(2,1)} fusion(f32[256,2688]{1,0:T(8,128)} %fusion.63, f32[256,2688]{1,0:T(8,128)} %convolution_add_fusion.1, bf16[2688,128]{1,0:T(8,128)(2,1)S(1)} %copy-done.12, f32[256,256]{0,1:T(8,128)S(1)} %copy-done.5), kind=kOutput, calls=%fused_computation.5 | convolution fusion | flops 178225152 | bytes 7634944 | tf_op jit(solution)/shard_map/dot_general | solution.py:35
  155.7 70.0 %all-reduce.6.cloned.1.call-done = (bf16[16,256]{1,0:T(8,128)(2,1)}, bf16[16,128]{1,0:T(8,128)(2,1)}, bf16[16,128]{1,0:T(8,128)(2,1)}, bf16[256,16]{0,1:T(8,128)(2,1)}, bf16[16,1344]{1,0:T(8,128)(2,1)}) async-done(((bf16[16,256]{1,0:T(8,128)(2,1)}, bf16[16,128]{1,0:T(8,128)(2,1)}, bf16[16,128]{1,0:T(8,128)(2,1)}, bf16[256,16]{0,1:T(8,128)(2,1)}, bf16[16,1344]{1,0:T(8,128)(2,1)}), ...) | async-done | bytes 67600 | tf_op jit(solution)/shard_map/psum | solution.py:234
  232.3 67.5 %all-reduce.4.cloned.1.call-done = bf16[1344,48]{0,1:T(8,128)(2,1)} async-done(((bf16[1344,48]{0,1:T(8,128)(2,1)}), bf16[1344,48]{0,1:T(8,128)(2,1)}) %all-reduce.4.cloned.1.call-update) | async-done | bytes 129040 | tf_op jit(solution)/shard_map/psum | solution.py:233
  301.4 8.7 %reduce-scatter.11.cloned.1.call-done = bf16[128,2688]{1,0:T(8,128)(2,1)} async-done(((bf16[256,2688]{1,0:T(8,128)(2,1)}), bf16[128,2688]{1,0:T(8,128)(2,1)}) %reduce-scatter.11.cloned.1.call-update) | async-done | bytes 688144 | tf_op jit(solution)/shard_map/reduce_scatter | solution.py:222
  (187 shorter events, 45.6 us)
Async XLA Ops:
  7.2 36.4 %copy-start = (bf16[2688,256]{1,0:T(8,128)(2,1)S(1)}, bf16[2688,256]{1,0:T(8,128)(2,1)}, u32[]{:S(2)}) copy-start(bf16[2688,256]{1,0:T(8,128)(2,1)} %param.26) | copy-start | bytes 4128772
  7.2 22.3 %all-gather.3.cloned.1.call-start = ((), (), s32[]{:S(2)}) async-start(), calls=%async_computation.4 | async-start | bytes 2064384 | tf_op jit(solution)/shard_map/all_gather | solution.py:88
  11.4 20.2 %copy-start.32 = (bf16[16,128]{1,0:T(8,128)(2,1)S(1)}, bf16[16,128]{1,0:T(8,128)(2,1)}, u32[]{:S(2)}) copy-start(bf16[16,128]{1,0:T(8,128)(2,1)} %param.32) | copy-start | bytes 12292
  11.4 20.4 %copy-start.7 = (bf16[2688,128]{1,0:T(8,128)(2,1)S(1)}, bf16[2688,128]{1,0:T(8,128)(2,1)}, u32[]{:S(2)}) copy-start(bf16[2688,128]{1,0:T(8,128)(2,1)} %param.27) | copy-start | bytes 2064388
  11.4 55.0 %reduce-scatter.13.cloned.1.call-start = ((), (), s32[]{:S(2)}) async-start(), calls=%async_computation.9 | async-start | bytes 98304
  12.2 14.8 %collective-permute-start.4 = (s32[256]{0:T(256)S(1)}, s32[256]{0:T(256)S(1)}, u32[]{:S(2)}, u32[]{:S(2)}) collective-permute-start(s32[256]{0:T(256)S(1)} %get-tuple-element.19), channel_id=1, source_target_pairs={{0,8},{2,10},{4,12},{6,14},{1,9},{3,11},{5,13},{7,15},{16,24},{18,... | collective-permute-start | bytes 3080 | tf_op jit(solution)/shard_map/ppermute | solution.py:15
  18.1 8.9 %collective-permute-start.5 = (s32[256]{0:T(256)S(1)}, s32[256]{0:T(256)S(1)}, u32[]{:S(2)}, u32[]{:S(2)}) collective-permute-start(s32[256]{0:T(256)S(1)} %get-tuple-element.19), channel_id=1, source_target_pairs={{0,6},{2,8},{4,10},{6,12},{8,14},{1,7},{3,9},{5,11},{7,13},{9,15},... | collective-permute-start | bytes 3080 | tf_op jit(solution)/shard_map/ppermute | solution.py:15
  22.5 4.5 %collective-permute-start.6 = (s32[256]{0:T(256)S(1)}, s32[256]{0:T(256)S(1)}, u32[]{:S(2)}, u32[]{:S(2)}) collective-permute-start(s32[256]{0:T(256)S(1)} %get-tuple-element.19), channel_id=1, source_target_pairs={{0,4},{2,6},{4,8},{6,10},{8,12},{10,14},{1,5},{3,7},{5,9},{7,11},{... | collective-permute-start | bytes 3080 | tf_op jit(solution)/shard_map/ppermute | solution.py:15
  23.8 4.4 %collective-permute-start.7 = (s32[256]{0:T(256)S(1)}, s32[256]{0:T(256)S(1)}, u32[]{:S(2)}, u32[]{:S(2)}) collective-permute-start(s32[256]{0:T(256)S(1)} %get-tuple-element.19), channel_id=1, source_target_pairs={{0,2},{2,4},{4,6},{6,8},{8,10},{10,12},{12,14},{1,3},{3,5},{5,7},{... | collective-permute-start | bytes 3080 | tf_op jit(solution)/shard_map/ppermute | solution.py:15
  27.0 24.3 %copy-start.34 = (f32[256]{0:T(256)}, f32[256]{0:T(256)S(1)}, u32[]{:S(2)}) copy-start(f32[256]{0:T(256)S(1)} %fusion.70) | copy-start | bytes 3076
  33.5 10.9 %collective-permute-start = (bf16[256,256]{0,1:T(8,128)(2,1)S(1)}, bf16[256,256]{0,1:T(8,128)(2,1)S(1)}, u32[]{:S(2)}, u32[]{:S(2)}) collective-permute-start(bf16[256,256]{0,1:T(8,128)(2,1)S(1)} %pad_maximum_fusion.1), channel_id=1, source_target_pairs={{0,8},{2,10},{4,12},{6,14},{1,9},{3,11},{5,13},{7,15},{16,24},{18,... | collective-permute-start | bytes 393224 | tf_op jit(solution)/shard_map/ppermute | solution.py:15
  37.4 7.7 %collective-permute-start.1 = (bf16[256,256]{0,1:T(8,128)(2,1)S(1)}, bf16[256,256]{0,1:T(8,128)(2,1)S(1)}, u32[]{:S(2)}, u32[]{:S(2)}) collective-permute-start(bf16[256,256]{0,1:T(8,128)(2,1)S(1)} %pad_maximum_fusion.1), channel_id=1, source_target_pairs={{0,6},{2,8},{4,10},{6,12},{8,14},{1,7},{3,9},{5,11},{7,13},{9,15},... | collective-permute-start | bytes 393224 | tf_op jit(solution)/shard_map/ppermute | solution.py:15
  38.7 7.1 %collective-permute-start.2 = (bf16[256,256]{0,1:T(8,128)(2,1)S(1)}, bf16[256,256]{0,1:T(8,128)(2,1)S(1)}, u32[]{:S(2)}, u32[]{:S(2)}) collective-permute-start(bf16[256,256]{0,1:T(8,128)(2,1)S(1)} %pad_maximum_fusion.1), channel_id=1, source_target_pairs={{0,4},{2,6},{4,8},{6,10},{8,12},{10,14},{1,5},{3,7},{5,9},{7,11},{... | collective-permute-start | bytes 393224 | tf_op jit(solution)/shard_map/ppermute | solution.py:15
  40.5 5.9 %collective-permute-start.3 = (bf16[256,256]{0,1:T(8,128)(2,1)S(1)}, bf16[256,256]{0,1:T(8,128)(2,1)S(1)}, u32[]{:S(2)}, u32[]{:S(2)}) collective-permute-start(bf16[256,256]{0,1:T(8,128)(2,1)S(1)} %pad_maximum_fusion.1), channel_id=1, source_target_pairs={{0,2},{2,4},{4,6},{6,8},{8,10},{10,12},{12,14},{1,3},{3,5},{5,7},{... | collective-permute-start | bytes 393224 | tf_op jit(solution)/shard_map/ppermute | solution.py:15
  54.4 24.2 %reduce-scatter.9.cloned.1.call-start = ((), (), s32[]{:S(2)}) async-start(), calls=%async_computation.5 | async-start | bytes 2064384 | tf_op jit(solution)/shard_map/reduce_scatter | solution.py:141
  57.5 21.2 %copy-start.20 = (bf16[16,2688]{1,0:T(8,128)(2,1)S(1)}, bf16[16,2688]{1,0:T(8,128)(2,1)}, u32[]{:S(2)}) copy-start(bf16[16,2688]{1,0:T(8,128)(2,1)} %param.35) | copy-start | bytes 258052
  57.5 22.7 %copy-start.9 = (bf16[128,2688]{1,0:T(8,128)(2,1)S(1)}, bf16[128,2688]{1,0:T(8,128)(2,1)}, u32[]{:S(2)}) copy-start(bf16[128,2688]{1,0:T(8,128)(2,1)} %param.19) | copy-start | bytes 2064388
  57.5 35.6 %all-gather.5.cloned.1.call-start = ((), (), s32[]{:S(2)}) async-start(), calls=%async_computation.6 | async-start | bytes 2064384 | tf_op jit(solution)/shard_map/all_gather | solution.py:158
  82.2 67.3 %reduce-scatter.15.cloned.1.call-start = ((), (), s32[]{:S(2)}) async-start(), calls=%async_computation.10 | async-start | bytes 1032192
  115.0 8.7 %collective-permute-start.10 = (bf16[256,256]{0,1:T(8,128)(2,1)S(1)}, bf16[256,256]{0,1:T(8,128)(2,1)S(1)}, u32[]{:S(2)}, u32[]{:S(2)}) collective-permute-start(bf16[256,256]{0,1:T(8,128)(2,1)S(1)} %get-tuple-element.17), channel_id=1, source_target_pairs={{6,0},{8,2},{10,4},{12,6},{14,8},{7,1},{9,3},{11,5},{13,7},{15,9},... | collective-permute-start | bytes 393224 | tf_op jit(solution)/shard_map/ppermute | solution.py:15
  116.4 17.4 %collective-permute-start.11 = (bf16[256,256]{0,1:T(8,128)(2,1)S(1)}, bf16[256,256]{0,1:T(8,128)(2,1)S(1)}, u32[]{:S(2)}, u32[]{:S(2)}) collective-permute-start(bf16[256,256]{0,1:T(8,128)(2,1)S(1)} %get-tuple-element.16), channel_id=1, source_target_pairs={{8,0},{10,2},{12,4},{14,6},{9,1},{11,3},{13,5},{15,7},{24,16},{26,... | collective-permute-start | bytes 393224 | tf_op jit(solution)/shard_map/ppermute | solution.py:15
  117.7 16.1 %collective-permute-start.8 = (bf16[256,256]{0,1:T(8,128)(2,1)S(1)}, bf16[256,256]{0,1:T(8,128)(2,1)S(1)}, u32[]{:S(2)}, u32[]{:S(2)}) collective-permute-start(bf16[256,256]{0,1:T(8,128)(2,1)S(1)} %get-tuple-element.15), channel_id=1, source_target_pairs={{2,0},{4,2},{6,4},{8,6},{10,8},{12,10},{14,12},{3,1},{5,3},{7,5},{... | collective-permute-start | bytes 393224 | tf_op jit(solution)/shard_map/ppermute | solution.py:15
  119.0 14.9 %copy-start.15 = (f32[256,128]{0,1:T(8,128)S(1)}, f32[256,128]{0,1:T(8,128)}, u32[]{:S(2)}) copy-start(f32[256,128]{0,1:T(8,128)} %copy-done.14) | copy-start | bytes 393220
  119.0 14.9 %copy-start.41 = (f32[128]{0:T(128)S(1)}, f32[128]{0:T(128)}, u32[]{:S(2)}) copy-start(f32[128]{0:T(128)} %param.24) | copy-start | bytes 1540
  119.0 14.8 %collective-permute-start.9 = (bf16[256,256]{0,1:T(8,128)(2,1)S(1)}, bf16[256,256]{0,1:T(8,128)(2,1)S(1)}, u32[]{:S(2)}, u32[]{:S(2)}) collective-permute-start(bf16[256,256]{0,1:T(8,128)(2,1)S(1)} %get-tuple-element.18), channel_id=1, source_target_pairs={{4,0},{6,2},{8,4},{10,6},{12,8},{14,10},{5,1},{7,3},{9,5},{11,7},{... | collective-permute-start | bytes 393224 | tf_op jit(solution)/shard_map/ppermute | solution.py:15
  121.7 13.4 %copy-start.33 = (bf16[16,128]{1,0:T(8,128)(2,1)S(1)}, bf16[16,128]{1,0:T(8,128)(2,1)}, u32[]{:S(2)}) copy-start(bf16[16,128]{1,0:T(8,128)(2,1)} %param.32) | copy-start | bytes 12292
  139.0 86.7 %all-reduce.6.cloned.1.call-start = ((), (), s32[]{:S(2)}) async-start(), calls=%async_computation.11 | async-start | bytes 139264 | tf_op jit(solution)/shard_map/psum | solution.py:234
  143.7 156.0 %all-reduce.4.cloned.1.call-start = ((), (), s32[]{:S(2)}) async-start(), calls=%async_computation.8 | async-start | bytes 270336 | tf_op jit(solution)/shard_map/psum | solution.py:233
  151.3 158.8 %reduce-scatter.11.cloned.1.call-start = ((), (), s32[]{:S(2)}) async-start(), calls=%async_computation.7 | async-start | bytes 2064384 | tf_op jit(solution)/shard_map/reduce_scatter | solution.py:222
  155.6 154.5 %copy-start.2 = (bf16[128,2688]{1,0:T(8,128)(2,1)S(1)}, bf16[128,2688]{1,0:T(8,128)(2,1)}, u32[]{:S(2)}) copy-start(bf16[128,2688]{1,0:T(8,128)(2,1)} %param.18) | copy-start | bytes 2064388
  155.6 154.5 %copy-start.22 = (f32[2688]{0:T(1024)S(1)}, f32[2688]{0:T(1024)}, u32[]{:S(2)}) copy-start(f32[2688]{0:T(1024)} %param.22) | copy-start | bytes 32260
  155.6 154.5 %copy-start.39 = (f32[128]{0:T(128)S(1)}, f32[128]{0:T(128)}, u32[]{:S(2)}) copy-start(f32[128]{0:T(128)} %copy-done.38) | copy-start | bytes 1540
  (33 other events, 136.9 us)
Sparse Core Ops, SparseCore 0:
  11.5 12.2 all-gather.2
  54.6 11.7 reduce-scatter.12
  68.6 9.9 reduce-scatter.8
  82.3 10.7 all-gather.4
  139.1 10.3 reduce-scatter.14
  154.5 71.0 all-reduce.5
  230.0 69.7 all-reduce.3
  302.0 8.0 reduce-scatter.10
where the time goes:
time: 321 us; the launch traced here: 320 us
  waiting for transfers between devices  188 us (59%)
  matrix products  51.8 us (16%)
  starting transfers between devices  30.5 us (10%)
  other arithmetic  20.1 us (6%)
  between operations  15.6 us (5%)
  local copies, waits for them, and re-layouts  9.76 us (3%)
  blocking collectives  3.64 us (1%)
    psum x1, waiting for transfers between devices, on_device(): lax.psum(query_up_contribution.astype(jnp.bfloat16), 'ctx')  70 us
    psum x1, waiting for transfers between devices, on_device(): lax.psum(down_term, 'ctx').astype(jnp.float32)  67.5 us
    ppermute x12, starting transfers between devices, passed_along(): lax.ppermute(value, axis, [(source, source + steps) for source in range(l...  30.2 us
    dot_general x10, matrix products, multiply_by_transpose(): lax.dot_general(first_op, second_op, (((1,), (1,)), ((), ())), preferred_...  16.7 us
    ppermute x12, waiting for transfers between devices, passed_along(): lax.ppermute(value, axis, [(source, source + steps) for source in range(l...  13.4 us
    unnamed x10, waiting for transfers between devices  12.5 us
    reduce_scatter x1, waiting for transfers between devices, on_device(): lax.psum_scatter(part_out.astype(jnp.bfloat16), 'tp', scatter_dimension=0...  12.3 us
    unnamed x102, local copies, waits for them, and re-layouts  9.72 us
  transfers between devices with their start and end apart: 20, of which 10 were waited for; matrix products, arithmetic and copies ran while one was open for 10% of the time, Pallas kernels for 0%

commit v1 on v0

--- a/solution.py
+++ b/solution.py
@@ -230,7 +230,7 @@
         tiled=True,
     )
     adapter_totals = (
-        lax.psum(down_term, "ctx").astype(jnp.float32),
+        jnp.sum(lax.all_gather(down_term, "ctx"), axis=0).astype(jnp.float32),
         lax.psum(query_up_contribution.astype(jnp.bfloat16), "ctx").astype(jnp.float32),
         lax.psum(key_up_contribution.astype(jnp.bfloat16), "ctx").astype(jnp.float32),
         lax.psum(value_up_contribution.astype(jnp.bfloat16), "ctx").astype(jnp.float32),

time: 321 us -> 273 us (0.85)
  waiting for transfers between devices: 188 us -> 110 us
  blocking collectives: 3.64 us -> 39.2 us
  matrix products: 51.8 us -> 48 us
    psum x1 -> x0, waiting for transfers between devices: 67.5 us -> none  [on_device(): lax.psum(down_term, 'ctx').astype(jnp.float32)]
    all_gather x0 -> x1, blocking collectives: none -> 35.5 us  [on_device(): lax.all_gather(down_term, 'ctx')]
    reduce_scatter x1, waiting for transfers between devices: 8.71 us -> 0.01 us  [on_device(): lax.psum_scatter(grad_normed.astype(jnp.bfloat16), 'tp', scatter_dimensio...]
    unnamed x102 -> x98, local copies, waits for them, and re-layouts: 9.72 us -> 8.45 us
    unnamed x10 -> x9, waiting for transfers between devices: 12.5 us -> 13.3 us
  transfers between devices with their start and end apart: 20 -> 19, of which waited for: 10 -> 8; matrix products, arithmetic and copies ran while one was open for 10% -> 9% of each run, Pallas kernels for 0% -> 0%
where the time goes in v1:
time: 273 us; the launch traced here: 272 us
  waiting for transfers between devices  110 us (40%)
  matrix products  48 us (18%)
  blocking collectives  39.2 us (14%)
  starting transfers between devices  30.5 us (11%)
  other arithmetic  20.6 us (8%)
  between operations  15.6 us (6%)
  local copies, waits for them, and re-layouts  8.49 us (3%)
    psum x1, waiting for transfers between devices, on_device(): lax.psum(query_up_contribution.astype(jnp.bfloat16), 'ctx')  67 us
    all_gather x1, blocking collectives, on_device(): lax.all_gather(down_term, 'ctx')  35.5 us
    ppermute x12, starting transfers between devices, passed_along(): lax.ppermute(value, axis, [(source, source + steps) for source in range(l...  30.2 us
    dot_general x10, matrix products, multiply_by_transpose(): lax.dot_general(first_op, second_op, (((1,), (1,)), ((), ())), preferred_...  13.6 us
    ppermute x12, waiting for transfers between devices, passed_along(): lax.ppermute(value, axis, [(source, source + steps) for source in range(l...  13.4 us
    unnamed x9, waiting for transfers between devices  13.3 us
    reduce_scatter x1, waiting for transfers between devices, on_device(): lax.psum_scatter(part_out.astype(jnp.bfloat16), 'tp', scatter_dimension=0...  12.3 us
    dot_general x10, matrix products, matrix_product(): return jnp.dot(first_op, second_op, preferred_element_type=jnp.float32)  9.23 us
  transfers between devices with their start and end apart: 19, of which 8 were waited for; matrix products, arithmetic and copies ran while one was open for 9% of the time, Pallas kernels for 0%

profile of v1, /device:TPU:0, one launch (start us, length us, event | category | flops | bytes accessed | tf_op | source)
XLA Modules:
  0.0 272.2 jit_solution(12515186945032035979)
XLA Ops:
  8.7 2.2 fusion.21
  11.7 5.9 %collective-permute-start.4 = (s32[256]{0:T(256)S(1)}, s32[256]{0:T(256)S(1)}, u32[]{:S(2)}, u32[]{:S(2)}) collective-permute-start(s32[256]{0:T(256)S(1)} %get-tuple-element.19), channel_id=1, source_target_pairs={{0,8},{2,10},{4,12},{6,14},{1,9},{3,11},{5,13},{7,15},{16,24},{18,... | collective-permute-start | bytes 3080 | tf_op jit(solution)/shard_map/ppermute | solution.py:15
  17.6 4.4 %collective-permute-start.5 = (s32[256]{0:T(256)S(1)}, s32[256]{0:T(256)S(1)}, u32[]{:S(2)}, u32[]{:S(2)}) collective-permute-start(s32[256]{0:T(256)S(1)} %get-tuple-element.19), channel_id=1, source_target_pairs={{0,6},{2,8},{4,10},{6,12},{8,14},{1,7},{3,9},{5,11},{7,13},{9,15},... | collective-permute-start | bytes 3080 | tf_op jit(solution)/shard_map/ppermute | solution.py:15
  23.3 3.1 %collective-permute-start.7 = (s32[256]{0:T(256)S(1)}, s32[256]{0:T(256)S(1)}, u32[]{:S(2)}, u32[]{:S(2)}) collective-permute-start(s32[256]{0:T(256)S(1)} %get-tuple-element.19), channel_id=1, source_target_pairs={{0,2},{2,4},{4,6},{6,8},{8,10},{10,12},{12,14},{1,3},{3,5},{5,7},{... | collective-permute-start | bytes 3080 | tf_op jit(solution)/shard_map/ppermute | solution.py:15
  29.0 2.0 convolution_convert_fusion.2
  32.9 3.9 %collective-permute-start = (bf16[256,256]{0,1:T(8,128)(2,1)S(1)}, bf16[256,256]{0,1:T(8,128)(2,1)S(1)}, u32[]{:S(2)}, u32[]{:S(2)}) collective-permute-start(bf16[256,256]{0,1:T(8,128)(2,1)S(1)} %pad_maximum_fusion.1), channel_id=1, source_target_pairs={{0,8},{2,10},{4,12},{6,14},{1,9},{3,11},{5,13},{7,15},{16,24},{18,... | collective-permute-start | bytes 393224 | tf_op jit(solution)/shard_map/ppermute | solution.py:15
  38.2 1.9 collective-permute-start.2
  40.0 2.8 %collective-permute-start.3 = (bf16[256,256]{0,1:T(8,128)(2,1)S(1)}, bf16[256,256]{0,1:T(8,128)(2,1)S(1)}, u32[]{:S(2)}, u32[]{:S(2)}) collective-permute-start(bf16[256,256]{0,1:T(8,128)(2,1)S(1)} %pad_maximum_fusion.1), channel_id=1, source_target_pairs={{0,2},{2,4},{4,6},{6,8},{8,10},{10,12},{12,14},{1,3},{3,5},{5,7},{... | collective-permute-start | bytes 393224 | tf_op jit(solution)/shard_map/ppermute | solution.py:15
  47.3 3.4 %fusion.31 = f32[2,256,1280]{1,2,0:T(8,128)} fusion(pred[256,1280]{0,1:T(8,128)(4,1)S(1)} %copy-done.21, bf16[1280,256]{0,1:T(8,128)(2,1)} %constant_dynamic-update-slice_fusion, f32[256,256]{0,1:T(8,128)S(1)} %get-tuple-element.24, f32[128]{0:T(128)S(1)} %copy-done.41, f32[256,2]{0,1:T(2,128)S(1)} %add_rsqrt_fusion), kind=kOutput, calls=%fused_computation.49 | convolution fusion | flops 169936640 | bytes 3541504 | tf_op jit(solution)/shard_map/div | solution.py:128
  50.7 2.2 fusion.46
  54.0 3.0 %convolution_convert_fusion = bf16[256,2688]{1,0:T(8,128)(2,1)} fusion(bf16[256,256]{0,1:T(8,128)(2,1)S(1)} %bitcast.91, bf16[256,2688]{1,0:T(8,128)(2,1)} %param.29), kind=kOutput, calls=%fused_computation.4 | convolution fusion | flops 353009664 | bytes 2883584 | tf_op jit(solution)/shard_map/dot_general | solution.py:31
  57.0 8.8 %reduce-scatter.13.cloned.1.call-done = bf16[128,16]{1,0:T(8,128)(2,1)} async-done(((bf16[256,16]{1,0:T(8,128)(2,1)}), bf16[128,16]{1,0:T(8,128)(2,1)}) %reduce-scatter.13.cloned.1.call-update) | async-done | bytes 4112
  65.8 12.3 %reduce-scatter.9.cloned.1.call-done = bf16[128,2688]{1,0:T(8,128)(2,1)} async-done(((bf16[256,2688]{1,0:T(8,128)(2,1)}), bf16[128,2688]{1,0:T(8,128)(2,1)}) %reduce-scatter.9.cloned.1.call-update) | async-done | bytes 688144 | tf_op jit(solution)/shard_map/reduce_scatter | solution.py:141
  78.1 1.6 multiply_reduce_fusion.2
  80.1 1.5 multiply_convert_fusion
  82.5 1.8 all_gather.23
  85.7 1.9 all_gather.20
  88.6 4.0 %all-gather.7.cloned.1.call-done = bf16[256,2688]{1,0:T(8,128)(2,1)} async-done(((bf16[128,2688]{1,0:T(8,128)(2,1)}), bf16[256,2688]{1,0:T(8,128)(2,1)}) %all-gather.7.cloned.1.call-update) | async-done | bytes 1376272 | tf_op jit(solution)/shard_map/all_gather | solution.py:158
  92.6 2.3 fusion.45
  94.9 3.2 %convolution_bitcast_fusion = f32[2,256,1280]{1,2,0:T(8,128)} fusion(bf16[256,2,128]{0,2,1:T(8,128)(2,1)S(1)} %bitcast.96, bf16[1280,256]{0,1:T(8,128)(2,1)} %constant_dynamic-update-slice_fusion), kind=kOutput, calls=%fused_computation.13 | convolution fusion | flops 167772160 | bytes 3080192 | tf_op jit(solution)/shard_map/thd,sd->hts/dot_general | solution.py:172
  98.8 5.7 %multiply_reduce_fusion.3 = (f32[256,2]{0,1:T(2,128)S(1)}, f32[256,2,128]{0,2,1:T(8,128)}) fusion(f32[256,256]{0,1:T(8,128)} %copy-done.18, f32[256,2]{0,1:T(2,128)S(1)} %copy-done.35, f32[128]{0:T(128)S(1)} %copy-done.42, f32[2,256,1280]{1,2,0:T(8,128)} %fusion.31, f32[2,256,1280]{1,2,0:T(8,128)} %convolution_bitcast_fusion, ...), kind=kOutput, calls=%fused_computation.99 | convolution fusion | flops 171312384 | bytes 11342336 | tf_op jit(solution)/shard_map/hts,sd->thd/dot_general | solution.py:177
  104.4 5.7 %convolution_bitcast_fusion.2 = f32[1280,128]{0,1:T(8,128)} fusion(f32[2,256,1280]{1,2,0:T(8,128)} %fusion.31, f32[2,256,1280]{1,2,0:T(8,128)} %convolution_bitcast_fusion, f32[256,256]{0,1:T(8,128)} %copy-done.18, f32[128]{0:T(128)S(1)} %copy-done.42, f32[256,2]{0,1:T(2,128)S(1)} %copy-done.35), kind=kOutput, calls=%fused_computation.19 | convolution fusion | flops 171247360 | bytes 6162944 | tf_op jit(solution)/shard_map/hts,thd->sd/dot_general | solution.py:180
  112.2 2.1 fusion.83
  118.5 1.6 collective-permute-start.9
  121.2 2.0 collective-permute-done.10
  123.2 10.1 %collective-permute-done.11 = bf16[256,256]{0,1:T(8,128)(2,1)S(1)} collective-permute-done((bf16[256,256]{0,1:T(8,128)(2,1)S(1)}, bf16[256,256]{0,1:T(8,128)(2,1)S(1)}, u32[]{:S(2)}, u32[]{:S(2)}) %collective-permute-start.11) | collective-permute-done | bytes 131104 | tf_op jit(solution)/shard_map/ppermute | solution.py:15
  136.4 4.1 %convolution_add_fusion.1 = f32[256,2688]{1,0:T(8,128)} fusion(f32[256,2688]{1,0:T(8,128)} %fusion.83, bf16[256,128]{0,1:T(8,128)(2,1)S(1)} %multiply_convert_fusion.4, bf16[2688,128]{1,0:T(8,128)(2,1)} %param.27), kind=kOutput, calls=%fused_computation.2 | convolution fusion | flops 176848896 | bytes 6258688 | tf_op jit(solution)/shard_map/dot_general | solution.py:35
  144.1 1.6 fusion.2
  145.8 67.0 %all-reduce.3.cloned.1.call-done = (bf16[16,256]{1,0:T(8,128)(2,1)}, bf16[16,128]{1,0:T(8,128)(2,1)}, bf16[16,128]{1,0:T(8,128)(2,1)}, bf16[256,16]{0,1:T(8,128)(2,1)}, bf16[16,1344]{1,0:T(8,128)(2,1)}) async-done(((bf16[16,256]{1,0:T(8,128)(2,1)}, bf16[16,128]{1,0:T(8,128)(2,1)}, bf16[16,128]{1,0:T(8,128)(2,1)}, bf16[256,16]{0,1:T(8,128)(2,1)}, bf16[16,1344]{1,0:T(8,128)(2,1)}), ...) | async-done | bytes 67600 | tf_op jit(solution)/shard_map/psum | solution.py:234
  219.3 4.3 %reduce-scatter.15.cloned.1.call-done = bf16[1344,48]{1,0:T(8,128)(2,1)} async-done(((bf16[2688,48]{1,0:T(8,128)(2,1)}), bf16[1344,48]{1,0:T(8,128)(2,1)}) %reduce-scatter.15.cloned.1.call-update) | async-done | bytes 129040
  224.8 35.5 %all-gather.1 = bf16[8,1344,48]{1,2,0:T(8,128)(2,1)} all-gather(bf16[1,1344,48]{1,2,0:T(8,128)(2,1)S(1)} %bitcast.98), channel_id=2, replica_groups=mesh['groups'=2,'ctx'=8,'tp'=2] {'ctx'}, dimensions={0}, use_global_device_ids=true | all-gather | bytes 1161216 | tf_op jit(solution)/shard_map/all_gather | solution.py:233
  262.5 1.6 fusion.22
  (182 shorter events, 43.2 us)
Async XLA Ops:
  7.2 35.9 %copy-start = (bf16[2688,256]{1,0:T(8,128)(2,1)S(1)}, bf16[2688,256]{1,0:T(8,128)(2,1)}, u32[]{:S(2)}) copy-start(bf16[2688,256]{1,0:T(8,128)(2,1)} %param.26) | copy-start | bytes 4128772
  7.2 21.8 %all-gather.5.cloned.1.call-start = ((), (), s32[]{:S(2)}) async-start(), calls=%async_computation.4 | async-start | bytes 2064384 | tf_op jit(solution)/shard_map/all_gather | solution.py:88
  8.7 20.3 %copy-start.36 = (f32[128]{0:T(128)}, f32[128]{0:T(128)S(1)}, u32[]{:S(2)}) copy-start(f32[128]{0:T(128)S(1)} %add_rsqrt_fusion.3) | copy-start | bytes 1540
  10.8 20.2 %copy-start.28 = (bf16[16,128]{1,0:T(8,128)(2,1)S(1)}, bf16[16,128]{1,0:T(8,128)(2,1)}, u32[]{:S(2)}) copy-start(bf16[16,128]{1,0:T(8,128)(2,1)} %param.32) | copy-start | bytes 12292
  10.9 20.4 %copy-start.8 = (bf16[2688,128]{1,0:T(8,128)(2,1)S(1)}, bf16[2688,128]{1,0:T(8,128)(2,1)}, u32[]{:S(2)}) copy-start(bf16[2688,128]{1,0:T(8,128)(2,1)} %param.27) | copy-start | bytes 2064388
  10.9 55.0 %reduce-scatter.13.cloned.1.call-start = ((), (), s32[]{:S(2)}) async-start(), calls=%async_computation.8 | async-start | bytes 98304
  11.7 14.8 %collective-permute-start.4 = (s32[256]{0:T(256)S(1)}, s32[256]{0:T(256)S(1)}, u32[]{:S(2)}, u32[]{:S(2)}) collective-permute-start(s32[256]{0:T(256)S(1)} %get-tuple-element.19), channel_id=1, source_target_pairs={{0,8},{2,10},{4,12},{6,14},{1,9},{3,11},{5,13},{7,15},{16,24},{18,... | collective-permute-start | bytes 3080 | tf_op jit(solution)/shard_map/ppermute | solution.py:15
  17.6 8.9 %collective-permute-start.5 = (s32[256]{0:T(256)S(1)}, s32[256]{0:T(256)S(1)}, u32[]{:S(2)}, u32[]{:S(2)}) collective-permute-start(s32[256]{0:T(256)S(1)} %get-tuple-element.19), channel_id=1, source_target_pairs={{0,6},{2,8},{4,10},{6,12},{8,14},{1,7},{3,9},{5,11},{7,13},{9,15},... | collective-permute-start | bytes 3080 | tf_op jit(solution)/shard_map/ppermute | solution.py:15
  22.0 4.5 %collective-permute-start.6 = (s32[256]{0:T(256)S(1)}, s32[256]{0:T(256)S(1)}, u32[]{:S(2)}, u32[]{:S(2)}) collective-permute-start(s32[256]{0:T(256)S(1)} %get-tuple-element.19), channel_id=1, source_target_pairs={{0,4},{2,6},{4,8},{6,10},{8,12},{10,14},{1,5},{3,7},{5,9},{7,11},{... | collective-permute-start | bytes 3080 | tf_op jit(solution)/shard_map/ppermute | solution.py:15
  23.3 4.4 %collective-permute-start.7 = (s32[256]{0:T(256)S(1)}, s32[256]{0:T(256)S(1)}, u32[]{:S(2)}, u32[]{:S(2)}) collective-permute-start(s32[256]{0:T(256)S(1)} %get-tuple-element.19), channel_id=1, source_target_pairs={{0,2},{2,4},{4,6},{6,8},{8,10},{10,12},{12,14},{1,3},{3,5},{5,7},{... | collective-permute-start | bytes 3080 | tf_op jit(solution)/shard_map/ppermute | solution.py:15
  26.4 24.3 %copy-start.32 = (f32[256]{0:T(256)}, f32[256]{0:T(256)S(1)}, u32[]{:S(2)}) copy-start(f32[256]{0:T(256)S(1)} %fusion.70) | copy-start | bytes 3076
  32.9 10.9 %collective-permute-start = (bf16[256,256]{0,1:T(8,128)(2,1)S(1)}, bf16[256,256]{0,1:T(8,128)(2,1)S(1)}, u32[]{:S(2)}, u32[]{:S(2)}) collective-permute-start(bf16[256,256]{0,1:T(8,128)(2,1)S(1)} %pad_maximum_fusion.1), channel_id=1, source_target_pairs={{0,8},{2,10},{4,12},{6,14},{1,9},{3,11},{5,13},{7,15},{16,24},{18,... | collective-permute-start | bytes 393224 | tf_op jit(solution)/shard_map/ppermute | solution.py:15
  36.9 7.7 %collective-permute-start.1 = (bf16[256,256]{0,1:T(8,128)(2,1)S(1)}, bf16[256,256]{0,1:T(8,128)(2,1)S(1)}, u32[]{:S(2)}, u32[]{:S(2)}) collective-permute-start(bf16[256,256]{0,1:T(8,128)(2,1)S(1)} %pad_maximum_fusion.1), channel_id=1, source_target_pairs={{0,6},{2,8},{4,10},{6,12},{8,14},{1,7},{3,9},{5,11},{7,13},{9,15},... | collective-permute-start | bytes 393224 | tf_op jit(solution)/shard_map/ppermute | solution.py:15
  38.2 7.1 %collective-permute-start.2 = (bf16[256,256]{0,1:T(8,128)(2,1)S(1)}, bf16[256,256]{0,1:T(8,128)(2,1)S(1)}, u32[]{:S(2)}, u32[]{:S(2)}) collective-permute-start(bf16[256,256]{0,1:T(8,128)(2,1)S(1)} %pad_maximum_fusion.1), channel_id=1, source_target_pairs={{0,4},{2,6},{4,8},{6,10},{8,12},{10,14},{1,5},{3,7},{5,9},{7,11},{... | collective-permute-start | bytes 393224 | tf_op jit(solution)/shard_map/ppermute | solution.py:15
  40.0 5.9 %collective-permute-start.3 = (bf16[256,256]{0,1:T(8,128)(2,1)S(1)}, bf16[256,256]{0,1:T(8,128)(2,1)S(1)}, u32[]{:S(2)}, u32[]{:S(2)}) collective-permute-start(bf16[256,256]{0,1:T(8,128)(2,1)S(1)} %pad_maximum_fusion.1), channel_id=1, source_target_pairs={{0,2},{2,4},{4,6},{6,8},{8,10},{10,12},{12,14},{1,3},{3,5},{5,7},{... | collective-permute-start | bytes 393224 | tf_op jit(solution)/shard_map/ppermute | solution.py:15
  53.9 24.2 %reduce-scatter.9.cloned.1.call-start = ((), (), s32[]{:S(2)}) async-start(), calls=%async_computation.5 | async-start | bytes 2064384 | tf_op jit(solution)/shard_map/reduce_scatter | solution.py:141
  57.0 21.2 %copy-start.20 = (bf16[16,2688]{1,0:T(8,128)(2,1)S(1)}, bf16[16,2688]{1,0:T(8,128)(2,1)}, u32[]{:S(2)}) copy-start(bf16[16,2688]{1,0:T(8,128)(2,1)} %param.35) | copy-start | bytes 258052
  57.0 22.7 %copy-start.9 = (bf16[128,2688]{1,0:T(8,128)(2,1)S(1)}, bf16[128,2688]{1,0:T(8,128)(2,1)}, u32[]{:S(2)}) copy-start(bf16[128,2688]{1,0:T(8,128)(2,1)} %param.19) | copy-start | bytes 2064388
  57.0 35.6 %all-gather.7.cloned.1.call-start = ((), (), s32[]{:S(2)}) async-start(), calls=%async_computation.6 | async-start | bytes 2064384 | tf_op jit(solution)/shard_map/all_gather | solution.py:158
  81.7 131.1 %all-reduce.3.cloned.1.call-start = ((), (), s32[]{:S(2)}) async-start(), calls=%async_computation.10 | async-start | bytes 139264 | tf_op jit(solution)/shard_map/psum | solution.py:234
  114.5 8.7 %collective-permute-start.10 = (bf16[256,256]{0,1:T(8,128)(2,1)S(1)}, bf16[256,256]{0,1:T(8,128)(2,1)S(1)}, u32[]{:S(2)}, u32[]{:S(2)}) collective-permute-start(bf16[256,256]{0,1:T(8,128)(2,1)S(1)} %get-tuple-element.17), channel_id=1, source_target_pairs={{6,0},{8,2},{10,4},{12,6},{14,8},{7,1},{9,3},{11,5},{13,7},{15,9},... | collective-permute-start | bytes 393224 | tf_op jit(solution)/shard_map/ppermute | solution.py:15
  115.9 17.4 %collective-permute-start.11 = (bf16[256,256]{0,1:T(8,128)(2,1)S(1)}, bf16[256,256]{0,1:T(8,128)(2,1)S(1)}, u32[]{:S(2)}, u32[]{:S(2)}) collective-permute-start(bf16[256,256]{0,1:T(8,128)(2,1)S(1)} %get-tuple-element.16), channel_id=1, source_target_pairs={{8,0},{10,2},{12,4},{14,6},{9,1},{11,3},{13,5},{15,7},{24,16},{26,... | collective-permute-start | bytes 393224 | tf_op jit(solution)/shard_map/ppermute | solution.py:15
  117.2 16.1 %collective-permute-start.8 = (bf16[256,256]{0,1:T(8,128)(2,1)S(1)}, bf16[256,256]{0,1:T(8,128)(2,1)S(1)}, u32[]{:S(2)}, u32[]{:S(2)}) collective-permute-start(bf16[256,256]{0,1:T(8,128)(2,1)S(1)} %get-tuple-element.15), channel_id=1, source_target_pairs={{2,0},{4,2},{6,4},{8,6},{10,8},{12,10},{14,12},{3,1},{5,3},{7,5},{... | collective-permute-start | bytes 393224 | tf_op jit(solution)/shard_map/ppermute | solution.py:15
  118.5 14.9 %copy-start.15 = (f32[256,128]{0,1:T(8,128)S(1)}, f32[256,128]{0,1:T(8,128)}, u32[]{:S(2)}) copy-start(f32[256,128]{0,1:T(8,128)} %copy-done.14) | copy-start | bytes 393220
  118.5 14.9 %copy-start.39 = (f32[128]{0:T(128)S(1)}, f32[128]{0:T(128)}, u32[]{:S(2)}) copy-start(f32[128]{0:T(128)} %param.24) | copy-start | bytes 1540
  118.5 14.8 %collective-permute-start.9 = (bf16[256,256]{0,1:T(8,128)(2,1)S(1)}, bf16[256,256]{0,1:T(8,128)(2,1)S(1)}, u32[]{:S(2)}, u32[]{:S(2)}) collective-permute-start(bf16[256,256]{0,1:T(8,128)(2,1)S(1)} %get-tuple-element.18), channel_id=1, source_target_pairs={{4,0},{6,2},{8,4},{10,6},{12,8},{14,10},{5,1},{7,3},{9,5},{11,7},{... | collective-permute-start | bytes 393224 | tf_op jit(solution)/shard_map/ppermute | solution.py:15
  121.2 14.1 %copy-start.31 = (bf16[16,128]{1,0:T(8,128)(2,1)S(1)}, bf16[16,128]{1,0:T(8,128)(2,1)}, u32[]{:S(2)}) copy-start(bf16[16,128]{1,0:T(8,128)(2,1)} %param.33) | copy-start | bytes 12292
  140.5 83.2 %reduce-scatter.15.cloned.1.call-start = ((), (), s32[]{:S(2)}) async-start(), calls=%async_computation.9 | async-start | bytes 1032192
  142.0 120.5 %reduce-scatter.11.cloned.1.call-start = ((), (), s32[]{:S(2)}) async-start(), calls=%async_computation.7 | async-start | bytes 2064384 | tf_op jit(solution)/shard_map/reduce_scatter | solution.py:222
  224.8 37.7 %copy-start.2 = (bf16[128,2688]{1,0:T(8,128)(2,1)S(1)}, bf16[128,2688]{1,0:T(8,128)(2,1)}, u32[]{:S(2)}) copy-start(bf16[128,2688]{1,0:T(8,128)(2,1)} %param.18) | copy-start | bytes 2064388
  224.8 37.7 %copy-start.22 = (f32[2688]{0:T(1024)S(1)}, f32[2688]{0:T(1024)}, u32[]{:S(2)}) copy-start(f32[2688]{0:T(1024)} %param.22) | copy-start | bytes 32260
  224.8 37.7 %copy-start.37 = (f32[128]{0:T(128)S(1)}, f32[128]{0:T(128)}, u32[]{:S(2)}) copy-start(f32[128]{0:T(128)} %copy-done.36) | copy-start | bytes 1540
  (30 other events, 114.5 us)
Sparse Core Ops, SparseCore 0:
  11.0 12.2 all-gather.4
  54.0 11.7 reduce-scatter.12
  68.1 9.9 reduce-scatter.8
  81.8 10.7 all-gather.6
  140.6 72.1 all-reduce.2
  215.5 8.0 reduce-scatter.14
  226.0 9.9 reduce-scatter.10
